TPU v7x, 32 devices: a whole 2x2x4 slice. The times are simulated.
32 devices in a mesh: dp: 8 (over y, x, core), mp: 4 (over z).
Axes of the slice: x: 2, y: 2, z: 4, core: 2. Of those that a mesh axis runs over, the one named last changes fastest.
Arguments:
- activations: bfloat16 [4, 16, 1024, 4096], P(None, 'dp', 'mp'), may hold values from -6 to 6
- cotangents: bfloat16 [4, 16, 1024, 4096], P(None, 'dp', 'mp'), may hold values from -0.1875 to 0.1875
- lengths: int32 [16], P('dp'), may hold values from 128 to 1024, as said below
- project_in: bfloat16 [4, 64, 4096], replicated, may hold values from -0.09375 to 0.09375
- project_out: bfloat16 [4, 64, 4096], replicated, may hold values from -0.09375 to 0.09375
- preconditioner: bfloat16 [16384, 4096], P('mp', 'dp'), as said below
- queries: bfloat16 [8192, 16384], P('dp', 'mp'), may hold values from -0.0625 to 0.0625
Outputs:
- scores: float32 [16, 8192], P(None, ('dp', 'mp'))
Inputs may be any that keep to these rules, and one draw needn't show every extreme that they name: `lengths`: positions at or past an example's length are padding; some example has all 1024 positions live. `preconditioner`: each layer's 4096 x 4096 block is symmetric.
All inputs are finite; a program needn't handle non-finite values.
Results may differ from a plain program's by a relative error of at most 0.005.
Values may be sent and summed in bfloat16 or wider, within the bound.
No kernel may reach another device: no remote copies, remote signals or barrier semaphores. Data moves between devices by JAX's collectives and lax.ppermute only.
A program may use at most 128 MiB of HBM per device.

v0:
```python
import jax
import jax.numpy as jnp
from jax import lax
from jax.sharding import PartitionSpec as P


def split_parts(dense):
    upper = dense.astype(jnp.bfloat16)
    kept = lax.optimization_barrier(upper)
    lower = (dense - kept.astype(jnp.float32)).astype(jnp.bfloat16)
    return (upper, lower)


def body(activations, cotangents, lengths, project_in, project_out, preconditioner, queries):
    width_mp = lax.axis_size("mp")
    layer_count = activations.shape[0]
    tokens_here = activations.shape[2]
    factor_size = project_in.shape[1]
    block_size = factor_size * factor_size
    group_size = width_mp // layer_count
    mp_place = lax.axis_index("mp")
    contract = (((1,), (1,)), ((), ()))
    positions = mp_place * tokens_here + jnp.arange(tokens_here, dtype=jnp.int32)
    live_mask = positions[None, :] < lengths[:, None]
    left_factor = jnp.einsum(
        "lesd,lkd->lesk", activations, project_in, preferred_element_type=jnp.float32
    ).astype(jnp.bfloat16)
    right_factor = jnp.einsum(
        "lesd,lkd->lesk", cotangents, project_out, preferred_element_type=jnp.float32
    )
    right_factor = jnp.where(live_mask[None, :, :, None], right_factor, 0.0).astype(jnp.bfloat16)
    partial_grad = jnp.einsum(
        "lesj,lesc->eljc", right_factor, left_factor, preferred_element_type=jnp.float32
    )
    partial_grad = partial_grad.reshape(partial_grad.shape[0], layer_count * block_size)
    grad_total = lax.psum(partial_grad, "mp")
    layer_place = mp_place // group_size
    grad_layer = lax.dynamic_slice_in_dim(
        grad_total, layer_place * block_size, block_size, 1
    ).astype(jnp.bfloat16)
    spread = lax.all_to_all(grad_layer, "dp", split_axis=1, concat_axis=0, tiled=True)
    partial_pre = lax.dot_general(
        spread, preconditioner, contract, preferred_element_type=jnp.float32
    )
    precond_grad = lax.psum(partial_pre, "dp")
    upper_grad, lower_grad = split_parts(precond_grad)
    scores = lax.psum_scatter(
        lax.dot_general(queries, upper_grad, contract, preferred_element_type=jnp.float32)
        + lax.dot_general(queries, lower_grad, contract, preferred_element_type=jnp.float32),
        "mp",
        scatter_dimension=0,
        tiled=True,
    )
    return scores.T


def solution(mesh):
    return jax.shard_map(
        body,
        mesh=mesh,
        in_specs=(
            P(None, "dp", "mp", None),
            P(None, "dp", "mp", None),
            P("dp"),
            P(),
            P(),
            P("mp", "dp"),
            P("dp", "mp"),
        ),
        out_specs=P(None, ("dp", "mp")),
        check_vma=False,
    )
```

profile of v0, /device:TPU:0, one launch (start us, length us, event | category | flops | bytes accessed | tf_op | source)
XLA Modules:
  0.0 151.0 jit_solution(13580495785346025847)
XLA Ops:
  6.5 0.0 copy-start
  6.5 0.0 all-reduce.3.cloned.1.call-start
  6.5 0.9 broadcast_compare_fusion
  7.4 0.7 copy-done
  8.1 8.8 %fusion.16 = bf16[4,2,256,64]{2,3,0,1:T(8,128)(2,1)S(1)} fusion(bf16[4,64,4096]{2,1,0:T(8,128)(2,1)S(1)} %copy-done, bf16[4,2,256,4096]{3,2,1,0:T(8,128)(2,1)} %param.8, pred[2,256]{1,0:T(4,128)(4,1)S(1)} %broadcast_compare_fusion), kind=kOutput, calls=%fused_computation.8 | convolution fusion | flops 1074003968 | bytes 19137024 | tf_op jit(solution)/shard_map/lesd,lkd->lesk/dot_general | solution.py:28
  16.9 9.3 %fusion.24 = f32[2,4,64,64]{3,2,1,0:T(8,128)S(1)} fusion(bf16[4,2,256,64]{2,3,0,1:T(8,128)(2,1)S(1)} %fusion.16, bf16[4,64,4096]{2,1,0:T(8,128)(2,1)} %param.10, bf16[4,2,256,4096]{3,2,1,0:T(8,128)(2,1)} %param.7), kind=kOutput, calls=%fused_computation.11 | convolution fusion | flops 1090650112 | bytes 19267584 | tf_op jit(solution)/shard_map/lesj,lesc->eljc/dot_general | solution.py:32
  26.2 0.1 reshape.40
  26.3 23.0 %all-reduce.4 = bf16[2,16384]{1,0:T(2,128)(2,1)S(1)} all-reduce(f32[2,16384]{1,0:T(2,128)S(1)} %reshape.40), channel_id=1, replica_groups=mesh['dp'=8,'mp'=4] {'mp'}, use_global_device_ids=true, to_apply=%region_0.1 | all-reduce | flops 32768 | bytes 196608 | tf_op jit(solution)/shard_map/psum | solution.py:36
  49.4 8.3 %all_to_all.19 = bf16[2,8,512]{2,0,1:T(2,128)(2,1)S(1)} all-to-all(bf16[2,8,512]{2,0,1:T(2,128)(2,1)S(1)} %bitcast.27), channel_id=1, replica_groups=mesh['dp'=8,'mp'=4] {'dp'}, dimensions={1} | all-to-all | bytes 32768 | tf_op jit(solution)/shard_map/all_to_all | solution.py:41
  57.7 4.1 %fusion.27 = f32[16,4096]{1,0:T(8,128)} fusion(bf16[16,512]{1,0:T(8,128)(2,1)S(1)} %all_to_all.17, bf16[4096,512]{1,0:T(8,128)(2,1)} %param.12), kind=kOutput, calls=%fused_computation.16 | convolution fusion | flops 67108864 | bytes 4472832 | tf_op jit(solution)/shard_map/dot_general | solution.py:42
  61.7 0.0 all-reduce.3.cloned.1.call-update
  61.8 0.0 reduce-scatter.2.cloned.1.call-start
  61.8 50.5 %all-reduce.3.cloned.1.call-done = f32[16,4096]{1,0:T(8,128)} async-done(((f32[16,4096]{1,0:T(8,128)}), f32[16,4096]{1,0:T(8,128)}) %all-reduce.3.cloned.1.call-update) | async-done | bytes 262160 | tf_op jit(solution)/shard_map/psum | solution.py:45
  112.3 0.0 copy-start.1
  112.3 1.0 convert_element_type.21
  113.3 5.6 %fusion.28 = f32[16,1024]{1,0:T(8,128)S(1)} fusion(bf16[16,4096]{1,0:T(8,128)(2,1)S(1)} %convert_element_type.21, bf16[1024,4096]{1,0:T(8,128)(2,1)} %param.13), kind=kOutput, calls=%fused_computation.17 | convolution fusion | flops 134217728 | bytes 8585216 | tf_op jit(solution)/shard_map/dot_general | solution.py:48
  119.0 0.0 copy-done.1
  119.0 6.3 %fusion.21 = f32[1024,16]{0,1:T(8,128)} fusion(f32[16,1024]{1,0:T(8,128)S(1)} %fusion.28, bf16[1024,4096]{1,0:T(8,128)(2,1)} %param.13, f32[16,4096]{1,0:T(8,128)S(1)} %copy-done.1, bf16[16,4096]{1,0:T(8,128)(2,1)S(1)} %convert_element_type.21), kind=kOutput, calls=%fused_computation.10 | convolution fusion | flops 134430720 | bytes 8912896 | tf_op jit(solution)/shard_map/dot_general | solution.py:49
  125.3 0.0 reduce-scatter.2.cloned.1.call-update
  125.3 18.9 %reduce-scatter.2.cloned.1.call-done = f32[256,16]{0,1:T(8,128)} async-done(((f32[1024,16]{0,1:T(8,128)}), f32[256,16]{0,1:T(8,128)}) %reduce-scatter.2.cloned.1.call-update) | async-done | bytes 16400 | tf_op jit(solution)/shard_map/reduce_scatter | solution.py:47
  (3 shorter events, 0.0 us)
Async XLA Ops:
  6.5 1.6 %copy-start = (bf16[4,64,4096]{2,1,0:T(8,128)(2,1)S(1)}, bf16[4,64,4096]{2,1,0:T(8,128)(2,1)}, u32[]{:S(2)}) copy-start(bf16[4,64,4096]{2,1,0:T(8,128)(2,1)} %param.11) | copy-start | bytes 6291460
  6.5 105.8 %all-reduce.3.cloned.1.call-start = ((), (), s32[]{:S(2)}) async-start(), calls=%async_computation.2 | async-start | bytes 524288 | tf_op jit(solution)/shard_map/psum | solution.py:45
  61.8 82.4 %reduce-scatter.2.cloned.1.call-start = ((), (), s32[]{:S(2)}) async-start(), calls=%async_computation.3 | async-start | bytes 81920 | tf_op jit(solution)/shard_map/reduce_scatter | solution.py:47
  112.3 6.7 %copy-start.1 = (f32[16,4096]{1,0:T(8,128)S(1)}, f32[16,4096]{1,0:T(8,128)}, u32[]{:S(2)}) copy-start(f32[16,4096]{1,0:T(8,128)} %all-reduce.3.cloned.1.call-done) | copy-start | bytes 786436
Sparse Core Ops, SparseCore 0:
  61.9 50.3 all-reduce.2
  125.4 18.6 reduce-scatter.1
where the time goes:
time: 151 us
  waiting for transfers between devices  69.4 us (46%)
  matrix products  34.1 us (23%)
  blocking collectives  31.3 us (21%)
  between operations  13.4 us (9%)
  other arithmetic  1.91 us (1%)
    psum x1, waiting for transfers between devices, body(): precond_grad = lax.psum(partial_pre, 'dp')  50.5 us
    psum x1, blocking collectives, body(): grad_total = lax.psum(partial_grad, 'mp')  23 us
    reduce_scatter x1, waiting for transfers between devices, body(): lax.psum_scatter(lax.dot_general(queries, upper_grad, contract, preferred...  18.9 us
    dot_general x1, matrix products, body(): jnp.einsum('lesj,lesc->eljc', right_factor, left_factor, preferred_elemen...  9.26 us
    dot_general x1, matrix products, body(): jnp.einsum('lesd,lkd->lesk', cotangents, project_out, preferred_element_t...  8.75 us
    all_to_all x1, blocking collectives, body(): lax.all_to_all(grad_layer, 'dp', split_axis=1, concat_axis=0, tiled=True)  8.27 us
    dot_general x1, matrix products, body(): lax.dot_general(queries, lower_grad, contract, preferred_element_type=jnp...  6.3 us
    dot_general x1, matrix products, body(): lax.dot_general(queries, upper_grad, contract, preferred_element_type=jnp...  5.65 us
  transfers between devices with their start and end apart: 2, of which 2 were waited for; matrix products, arithmetic and copies ran while one was open for 0% of the time, Pallas kernels for 0%

commit v1 on v0

--- a/solution.py
+++ b/solution.py
@@ -42,7 +42,10 @@
     partial_pre = lax.dot_general(
         spread, preconditioner, contract, preferred_element_type=jnp.float32
     )
-    precond_grad = lax.psum(partial_pre, "dp")
+    divide_page_now = lambda mine_x, which_axis: lax.all_gather(mine_x, axis_name=which_axis).sum(
+        axis=0
+    )
+    precond_grad = divide_page_now(partial_pre, "dp")
     upper_grad, lower_grad = split_parts(precond_grad)
     scores = lax.psum_scatter(
         lax.dot_general(queries, upper_grad, contract, preferred_element_type=jnp.float32)

time: 151 us -> 127 us (0.84)
  waiting for transfers between devices: 69.4 us -> 43.9 us
    psum x1 -> x0, waiting for transfers between devices: 50.5 us -> none  [body(): precond_grad = lax.psum(partial_pre, 'dp')]
    all_gather x0 -> x1, waiting for transfers between devices: none -> 24.4 us  [body(): lax.all_gather(mine_x, axis_name=which_axis).sum(axis=0)]
    reduce_sum x0 -> x1, other arithmetic: none -> 1.72 us  [body(): lax.all_gather(mine_x, axis_name=which_axis).sum(axis=0)]
where the time goes in v1:
time: 127 us; the launch traced here: 126 us
  waiting for transfers between devices  43.9 us (35%)
  matrix products  34.1 us (27%)
  blocking collectives  31.3 us (25%)
  between operations  13.4 us (11%)
  other arithmetic  2.61 us (2%)
    all_gather x1, waiting for transfers between devices, body(): lax.all_gather(mine_x, axis_name=which_axis).sum(axis=0)  24.4 us
    psum x1, blocking collectives, body(): grad_total = lax.psum(partial_grad, 'mp')  23 us
    reduce_scatter x1, waiting for transfers between devices, body(): lax.psum_scatter(lax.dot_general(queries, upper_grad, contract, preferred...  19.5 us
    dot_general x1, matrix products, body(): jnp.einsum('lesj,lesc->eljc', right_factor, left_factor, preferred_elemen...  9.26 us
    dot_general x1, matrix products, body(): jnp.einsum('lesd,lkd->lesk', cotangents, project_out, preferred_element_t...  8.75 us
    all_to_all x1, blocking collectives, body(): lax.all_to_all(grad_layer, 'dp', split_axis=1, concat_axis=0, tiled=True)  8.27 us
    dot_general x1, matrix products, body(): lax.dot_general(queries, lower_grad, contract, preferred_element_type=jnp...  6.29 us
    dot_general x1, matrix products, body(): lax.dot_general(queries, upper_grad, contract, preferred_element_type=jnp...  5.65 us
  transfers between devices with their start and end apart: 2, of which 2 were waited for; matrix products, arithmetic and copies ran while one was open for 0% of the time, Pallas kernels for 0%

profile of v1, /device:TPU:0, one launch (start us, length us, event | category | flops | bytes accessed | tf_op | source)
XLA Modules:
  0.0 126.2 jit_solution(11173350082605507123)
XLA Ops:
  6.5 0.0 copy-start
  6.5 0.0 all-gather.3.cloned.1.call-start
  6.5 0.9 broadcast_compare_fusion
  7.4 0.7 copy-done
  8.1 8.8 %fusion.16 = bf16[4,2,256,64]{2,3,0,1:T(8,128)(2,1)S(1)} fusion(bf16[4,64,4096]{2,1,0:T(8,128)(2,1)S(1)} %copy-done, bf16[4,2,256,4096]{3,2,1,0:T(8,128)(2,1)} %param.8, pred[2,256]{1,0:T(4,128)(4,1)S(1)} %broadcast_compare_fusion), kind=kOutput, calls=%fused_computation.8 | convolution fusion | flops 1074003968 | bytes 19137024 | tf_op jit(solution)/shard_map/lesd,lkd->lesk/dot_general | solution.py:28
  16.9 9.3 %fusion.24 = f32[2,4,64,64]{3,2,1,0:T(8,128)S(1)} fusion(bf16[4,2,256,64]{2,3,0,1:T(8,128)(2,1)S(1)} %fusion.16, bf16[4,64,4096]{2,1,0:T(8,128)(2,1)} %param.10, bf16[4,2,256,4096]{3,2,1,0:T(8,128)(2,1)} %param.7), kind=kOutput, calls=%fused_computation.11 | convolution fusion | flops 1090650112 | bytes 19267584 | tf_op jit(solution)/shard_map/lesj,lesc->eljc/dot_general | solution.py:32
  26.2 0.1 reshape.40
  26.3 23.0 %all-reduce.1 = bf16[2,16384]{1,0:T(2,128)(2,1)S(1)} all-reduce(f32[2,16384]{1,0:T(2,128)S(1)} %reshape.40), channel_id=1, replica_groups=mesh['dp'=8,'mp'=4] {'mp'}, use_global_device_ids=true, to_apply=%region_0.1 | all-reduce | flops 32768 | bytes 196608 | tf_op jit(solution)/shard_map/psum | solution.py:36
  49.4 8.3 %all_to_all.19 = bf16[2,8,512]{2,0,1:T(2,128)(2,1)S(1)} all-to-all(bf16[2,8,512]{2,0,1:T(2,128)(2,1)S(1)} %bitcast.29), channel_id=1, replica_groups=mesh['dp'=8,'mp'=4] {'dp'}, dimensions={1} | all-to-all | bytes 32768 | tf_op jit(solution)/shard_map/all_to_all | solution.py:41
  57.7 4.1 %fusion.27 = f32[16,4096]{1,0:T(8,128)} fusion(bf16[16,512]{1,0:T(8,128)(2,1)S(1)} %all_to_all.17, bf16[4096,512]{1,0:T(8,128)(2,1)} %param.12), kind=kOutput, calls=%fused_computation.16 | convolution fusion | flops 67108864 | bytes 4472832 | tf_op jit(solution)/shard_map/dot_general | solution.py:42
  61.8 0.0 all-gather.3.cloned.1.call-update
  61.8 0.0 reduce-scatter.2.cloned.1.call-start
  61.8 24.4 %all-gather.3.cloned.1.call-done = f32[128,4096]{1,0:T(8,128)} async-done(((f32[16,4096]{1,0:T(8,128)}), f32[128,4096]{1,0:T(8,128)}) %all-gather.3.cloned.1.call-update) | async-done | bytes 2097168 | tf_op jit(solution)/shard_map/all_gather | solution.py:45
  86.2 1.7 %reduce_sum.9 = f32[16,4096]{1,0:T(8,128)S(1)} reduce(f32[8,16,4096]{2,1,0:T(8,128)} %bitcast.28, f32[]{:T(128)} %constant.21.clone.1), dimensions={0}, to_apply=%region_1.2 | reduce | flops 458752 | bytes 2359300 | tf_op jit(solution)/shard_map/reduce_sum | solution.py:45
  88.0 5.6 %fusion.28 = f32[16,1024]{1,0:T(8,128)S(1)} fusion(bf16[16,4096]{1,0:T(8,128)(2,1)S(1)} %convert_element_type.21, bf16[1024,4096]{1,0:T(8,128)(2,1)} %param.13), kind=kOutput, calls=%fused_computation.17 | convolution fusion | flops 134217728 | bytes 8585216 | tf_op jit(solution)/shard_map/dot_general | solution.py:51
  93.6 6.3 %fusion.21 = f32[1024,16]{0,1:T(8,128)} fusion(f32[16,1024]{1,0:T(8,128)S(1)} %fusion.28, bf16[1024,4096]{1,0:T(8,128)(2,1)} %param.13, f32[16,4096]{1,0:T(8,128)S(1)} %reduce_sum.9, bf16[16,4096]{1,0:T(8,128)(2,1)S(1)} %convert_element_type.21), kind=kOutput, calls=%fused_computation.10 | convolution fusion | flops 134430720 | bytes 8912896 | tf_op jit(solution)/shard_map/dot_general | solution.py:52
  99.9 0.0 reduce-scatter.2.cloned.1.call-update
  99.9 19.5 %reduce-scatter.2.cloned.1.call-done = f32[256,16]{0,1:T(8,128)} async-done(((f32[1024,16]{0,1:T(8,128)}), f32[256,16]{0,1:T(8,128)}) %reduce-scatter.2.cloned.1.call-update) | async-done | bytes 16400 | tf_op jit(solution)/shard_map/reduce_scatter | solution.py:50
  (4 shorter events, 0.1 us)
Async XLA Ops:
  6.5 1.6 %copy-start = (bf16[4,64,4096]{2,1,0:T(8,128)(2,1)S(1)}, bf16[4,64,4096]{2,1,0:T(8,128)(2,1)}, u32[]{:S(2)}) copy-start(bf16[4,64,4096]{2,1,0:T(8,128)(2,1)} %param.11) | copy-start | bytes 6291460
  6.5 79.7 %all-gather.3.cloned.1.call-start = ((), (), s32[]{:S(2)}) async-start(), calls=%async_computation.3 | async-start | bytes 2359296 | tf_op jit(solution)/shard_map/all_gather | solution.py:45
  61.8 57.6 %reduce-scatter.2.cloned.1.call-start = ((), (), s32[]{:S(2)}) async-start(), calls=%async_computation.2 | async-start | bytes 81920 | tf_op jit(solution)/shard_map/reduce_scatter | solution.py:50
Sparse Core Ops, SparseCore 0:
  61.9 24.2 all-gather.2
  100.1 19.2 reduce-scatter.1
